TPU v7x, 32 devices: a whole 2x2x4 slice. The times are simulated.
32 devices in a mesh: dp: 8 (over z, y), ctx: 4 (over x, core).
Axes of the slice: x: 2, y: 2, z: 4, core: 2. Of those that a mesh axis runs over, the one named last changes fastest.
Arguments:
- queries: bfloat16 [4096, 4096], P(('dp', 'ctx')), may hold values from -40 to 40
- key_head_inputs: bfloat16 [4096, 512], P(('dp', 'ctx')), may hold values from -40 to 40
- value_head_inputs: bfloat16 [4096, 512], P(('dp', 'ctx')), may hold values from -6 to 6
- output_gradient: bfloat16 [4096, 4096], P(('dp', 'ctx')), may hold values from -6 to 6
- positions: int32 [4096], P(('dp', 'ctx')), may hold values from 0 to 1023, as said below
- counts: int32 [32], P(('dp', 'ctx')), may hold values from 64 to 128, as said below
- inputs: bfloat16 [4096, 8192], P(('dp', 'ctx')), may hold values from -6 to 6
Outputs:
- query_grad: bfloat16 [4096, 4096], P(('dp', 'ctx'))
- key_grad: bfloat16 [4096, 512], P(('dp', 'ctx'))
- value_grad: bfloat16 [4096, 512], P(('dp', 'ctx'))
- value_weight_gradient: float32 [512, 8192], P('dp', 'ctx')
Inputs may be any that keep to these rules, and one draw needn't show every extreme that they name: A device's valid slots are its first counts slots; the others are padding. Some device holds 128 valid slots. Along a sequence the positions of valid slots rise strictly; the first slot holds 0 and the last valid slot 1023. A padding slot repeats the position before it, or holds 1023 after the last valid slot.
All inputs are finite; a program needn't handle non-finite values.
Results may differ from a plain program's by a relative error of at most 0.0061.
Values may be sent and summed in bfloat16 or wider, within the bound.
No kernel may reach another device: no remote copies, remote signals or barrier semaphores. Data moves between devices by JAX's collectives and lax.ppermute only.
A program may use at most 128 MiB of HBM per device.

v0:
```python
import math
import jax
import jax.numpy as jnp
from jax import lax
from jax.sharding import PartitionSpec as P

HEAD_DIM = 128
QUERY_HEADS = 32
KEY_HEADS = 4
THETA = 500000.0


def rope_tables(position, head_size):
    half_width = head_size // 2
    frequency = jnp.exp(
        jnp.arange(half_width, dtype=jnp.float32) * (-2.0 * math.log(THETA) / head_size)
    )
    angles = position.astype(jnp.float32)[:, None] * frequency[None, :]
    return (jnp.cos(angles), jnp.sin(angles))


def apply_rotation(vectors, cosine_table, sine_lookup, sense):
    half_width = vectors.shape[-1] // 2
    lower_half = vectors[..., :half_width]
    upper_half = vectors[..., half_width:]
    cos_part = cosine_table[:, None, :]
    sin_part = sine_lookup[:, None, :] * sense
    return jnp.concatenate(
        [
            lower_half * cos_part - upper_half * sin_part,
            upper_half * cos_part + lower_half * sin_part,
        ],
        axis=-1,
    )


def per_device(
    queries, key_head_inputs, value_head_inputs, output_gradient, positions, counts, inputs
):
    row_number_total = queries.shape[0]
    query_group_width = QUERY_HEADS // KEY_HEADS
    axis_span = lax.axis_size("ctx")
    retained_slots = row_number_total * axis_span
    key_block = min(512, retained_slots)
    my_index = lax.axis_index("ctx")
    score_scale = 1.0 / math.sqrt(HEAD_DIM)
    cosine_table, sine_lookup = rope_tables(positions, HEAD_DIM)
    query_rotated = apply_rotation(
        queries.reshape(row_number_total, QUERY_HEADS, HEAD_DIM).astype(jnp.float32),
        cosine_table,
        sine_lookup,
        1.0,
    ).astype(jnp.bfloat16)
    key_rotated = apply_rotation(
        key_head_inputs.reshape(row_number_total, KEY_HEADS, HEAD_DIM).astype(jnp.float32),
        cosine_table,
        sine_lookup,
        1.0,
    ).astype(jnp.bfloat16)
    key_rotated = key_rotated.reshape(row_number_total, KEY_HEADS * HEAD_DIM)
    key_row_block, value_row_block, all_counts = (
        lax.all_gather(key_rotated, "ctx", axis=0, tiled=True),
        lax.all_gather(value_head_inputs, "ctx", axis=0, tiled=True),
        lax.all_gather(counts, "ctx", axis=0, tiled=True),
    )
    gathered_keys = key_row_block.reshape(retained_slots, KEY_HEADS, HEAD_DIM)
    gathered_values = value_row_block.reshape(retained_slots, KEY_HEADS, HEAD_DIM)
    key_valid = jnp.arange(retained_slots, dtype=jnp.int32) % row_number_total < jnp.repeat(
        all_counts, row_number_total
    )
    own_valid = jnp.arange(row_number_total, dtype=jnp.int32) < counts[0]
    initial_gradients = jnp.zeros((retained_slots, KEY_HEADS, HEAD_DIM), jnp.float32)
    first_slot = my_index * row_number_total
    key_accumulator = initial_gradients
    value_accumulator = initial_gradients
    query_count = query_rotated.shape[0]
    query_grouped = query_rotated.reshape(query_count, KEY_HEADS, query_group_width, HEAD_DIM)
    output_grad_grouped = output_gradient.reshape(
        query_count, KEY_HEADS, query_group_width, HEAD_DIM
    )
    q_slots = first_slot + jnp.arange(query_count, dtype=jnp.int32)
    block_total = (first_slot + query_count - 1) // key_block + 1

    def scores_for(begin_at):
        k_blk = lax.dynamic_slice_in_dim(gathered_keys, begin_at, key_block, 0)
        v_blk = lax.dynamic_slice_in_dim(gathered_values, begin_at, key_block, 0)
        k_slots = begin_at + jnp.arange(key_block, dtype=jnp.int32)
        k_valid = lax.dynamic_slice_in_dim(key_valid, begin_at, key_block, 0)
        allowed = own_valid[:, None] & k_valid[None, :] & (k_slots[None, :] <= q_slots[:, None])
        scores = (
            jnp.einsum("qhgd,khd->hgqk", query_grouped, k_blk, preferred_element_type=jnp.float32)
            * score_scale
        )
        d_probs = jnp.einsum(
            "qhgd,khd->hgqk", output_grad_grouped, v_blk, preferred_element_type=jnp.float32
        )
        return (k_blk, scores, d_probs, allowed)

    def first_pass(step_index, carry):
        row_top, row_total, weighted = carry
        k_blk, scores, d_probs, allowed = scores_for(step_index * key_block)
        new_top = jnp.maximum(row_top, jnp.max(jnp.where(allowed, scores, -1e30), axis=-1))
        factor = jnp.exp(row_top - new_top)
        exp_terms = jnp.where(allowed, jnp.exp(scores - new_top[..., None]), 0.0)
        return (
            new_top,
            row_total * factor + jnp.sum(exp_terms, axis=-1),
            weighted * factor + jnp.sum(exp_terms * d_probs, axis=-1),
        )

    statistic_shape = (KEY_HEADS, query_group_width, query_count)
    start_stats = (
        jnp.full(statistic_shape, -1e30, jnp.float32),
        jnp.zeros(statistic_shape, jnp.float32),
        jnp.zeros(statistic_shape, jnp.float32),
    )
    row_top, row_total, weighted = lax.fori_loop(0, block_total, first_pass, start_stats)
    row_total = jnp.where(own_valid[None, None, :], row_total, 1.0)
    row_delta = weighted / row_total

    def second_pass(step_index, carry):
        q_acc, key_sum, value_sum = carry
        begin_at = step_index * key_block
        k_blk, scores, d_probs, allowed = scores_for(begin_at)
        softmax = (
            jnp.where(allowed, jnp.exp(scores - row_top[..., None]), 0.0) / row_total[..., None]
        )
        d_scores = softmax * (d_probs - row_delta[..., None]) * score_scale
        prob_bf = softmax.astype(jnp.bfloat16)
        dscore_bf = d_scores.astype(jnp.bfloat16)
        q_acc = q_acc + jnp.einsum(
            "hgqk,khd->qhgd", dscore_bf, k_blk, preferred_element_type=jnp.float32
        )
        k_piece = jnp.einsum(
            "hgqk,qhgd->khd", dscore_bf, query_grouped, preferred_element_type=jnp.float32
        )
        v_piece = jnp.einsum(
            "hgqk,qhgd->khd", prob_bf, output_grad_grouped, preferred_element_type=jnp.float32
        )
        key_sum = lax.dynamic_update_slice_in_dim(
            key_sum,
            lax.dynamic_slice_in_dim(key_sum, begin_at, key_block, 0) + k_piece,
            begin_at,
            0,
        )
        value_sum = lax.dynamic_update_slice_in_dim(
            value_sum,
            lax.dynamic_slice_in_dim(value_sum, begin_at, key_block, 0) + v_piece,
            begin_at,
            0,
        )
        return (q_acc, key_sum, value_sum)

    query_offset = jnp.zeros((query_count, KEY_HEADS, query_group_width, HEAD_DIM), jnp.float32)
    q_acc, key_accumulator, value_accumulator = lax.fori_loop(
        0, block_total, second_pass, (query_offset, key_accumulator, value_accumulator)
    )
    q_grad_rot, key_accumulator, value_accumulator = (
        q_acc.reshape(query_count, QUERY_HEADS, HEAD_DIM),
        key_accumulator,
        value_accumulator,
    )
    key_portion, value_part = (
        lax.psum_scatter(
            key_accumulator.reshape(retained_slots, KEY_HEADS * HEAD_DIM),
            "ctx",
            scatter_dimension=0,
            tiled=True,
        ),
        lax.psum_scatter(
            value_accumulator.reshape(retained_slots, KEY_HEADS * HEAD_DIM),
            "ctx",
            scatter_dimension=0,
            tiled=True,
        ),
    )
    query_grad = (
        apply_rotation(q_grad_rot, cosine_table, sine_lookup, -1.0)
        .astype(jnp.bfloat16)
        .reshape(row_number_total, QUERY_HEADS * HEAD_DIM)
    )
    key_grad = (
        apply_rotation(
            key_portion.reshape(row_number_total, KEY_HEADS, HEAD_DIM),
            cosine_table,
            sine_lookup,
            -1.0,
        )
        .astype(jnp.bfloat16)
        .reshape(row_number_total, KEY_HEADS * HEAD_DIM)
    )
    value_grad = value_part.astype(jnp.bfloat16)
    weight_part = lax.psum_scatter(
        lax.dot_general(
            inputs, value_grad, (((0,), (0,)), ((), ())), preferred_element_type=jnp.float32
        ),
        "ctx",
        scatter_dimension=0,
        tiled=True,
    )
    shares = lax.psum_scatter(weight_part, "dp", scatter_dimension=1, tiled=True)
    return (query_grad, key_grad, value_grad, shares.T)


def solution(mesh):
    placed = (
        P(("dp", "ctx"), None),
        P(("dp", "ctx"), None),
        P(("dp", "ctx"), None),
        P(("dp", "ctx"), None),
        P(("dp", "ctx")),
        P(("dp", "ctx")),
        P(("dp", "ctx"), None),
    )
    return jax.shard_map(
        per_device,
        mesh=mesh,
        in_specs=placed,
        out_specs=(
            P(("dp", "ctx"), None),
            P(("dp", "ctx"), None),
            P(("dp", "ctx"), None),
            P("dp", "ctx"),
        ),
        check_vma=False,
    )
```

profile of v0, /device:TPU:0, one launch (start us, length us, event | category | flops | bytes accessed | tf_op | source)
XLA Modules:
  0.0 355.9 jit_solution(10259633255239488766)
XLA Ops:
  7.2 0.0 reduce-scatter.7.cloned.1.call-start
  8.1 1.2 dynamic-slice
  9.3 0.8 dynamic-update-slice
  10.1 0.7 convert_element_type.43
  10.7 6.4 %all-reduce = s32[4]{0:T(128)S(1)} all-reduce(s32[4]{0:T(128)S(1)} %dynamic-update-slice), channel_id=1, replica_groups=mesh['dp'=8,'ctx'=4] {'ctx'}, use_global_device_ids=true, to_apply=%add | all-reduce | flops 4 | bytes 32
  17.1 0.8 broadcast_multiply_fusion
  17.9 0.1 copy.20
  18.0 0.1 copy.21
  18.1 1.0 copy.24
  19.1 1.0 copy.46
  20.2 6.6 %all_gather.10 = bf16[512,512]{0,1:T(8,128)(2,1)S(1)} all-gather(bf16[128,512]{0,1:T(8,128)(2,1)S(1)} %bitcast.175), channel_id=1, replica_groups=mesh['dp'=8,'ctx'=4] {'ctx'}, dimensions={0}, use_global_device_ids=true | all-gather | bytes 655360 | tf_op jit(solution)/shard_map/all_gather | solution.py:62
  26.8 1.0 copy.29
  27.8 7.3 %all_gather.11 = bf16[512,512]{0,1:T(8,128)(2,1)S(1)} all-gather(bf16[128,512]{0,1:T(8,128)(2,1)S(1)} %copy.24), channel_id=1, replica_groups=mesh['dp'=8,'ctx'=4] {'ctx'}, dimensions={0}, use_global_device_ids=true | all-gather | bytes 655360 | tf_op jit(solution)/shard_map/all_gather | solution.py:63
  35.1 1.0 copy.27
  36.1 1.6 copy.25
  37.7 1.3 copy.28
  39.1 1.4 convert_bitcast_fusion
  40.5 0.4 copy.50
  40.9 0.8 subtract_convert_fusion.1
  41.7 0.4 copy.22
  42.1 0.4 copy.23
  42.5 0.6 pad_maximum_fusion
  43.1 7.6 %while.30 = (s32[]{:T(128)}, f32[4,8,128]{2,1,0:T(8,128)S(1)}, f32[4,8,128]{2,1,0:T(8,128)S(1)}, f32[4,8,128]{2,1,0:T(8,128)S(1)}, s32[]{:T(128)}, /*index=5*/bf...) while((s32[]{:T(128)}, f32[4,8,128]{2,1,0:T(8,128)S(1)}, ...), condition=%wide.region_4.5_spmd.clone, body=%wide.region_0.4_spmd.clone.sunk | while | flops 1099120896 | bytes 35166692 | solution.py:117
  43.2 0.1 fusion.84
  43.2 0.6 iota_compare_fusion.5
  43.9 0.2 compare_and_fusion.4
  44.1 2.3 fusion.85
  46.5 1.8 fusion.87
  48.3 2.4 fusion.86
  50.8 1.1 broadcast_in_dim.66.clone
  51.8 1.0 broadcast_in_dim.66
  52.9 1.6 broadcast_in_dim.50
  54.5 12.8 %while.31 = (s32[]{:T(128)}, f32[128,4,8,128]{3,0,2,1:T(8,128)}, f32[512,4,128]{2,0,1:T(8,128)}, f32[512,4,128]{2,0,1:T(8,128)}, s32[]{:T(128)}, /*index=5*/bf16...) while((s32[]{:T(128)}, f32[128,4,8,128]{3,0,2,1:T(8,128)}, ...), condition=%wide.region_6.7_spmd.clone, body=%wide.region_5.6_spmd.clone.sunk | while | flops 2704478464 | bytes 94034632 | solution.py:155
  54.5 0.1 fusion.98
  54.5 0.6 iota_compare_fusion.6
  55.2 0.2 compare_and_fusion.5
  55.4 3.4 fusion.99
  58.8 1.3 fusion.102
  60.2 1.3 fusion.100
  61.5 0.3 copy-done.6
  61.8 1.5 fusion.101
  63.3 0.1 copy-done.1
  63.4 0.1 copy-done.5
  63.5 2.4 bitcast_add_fusion.2
  65.9 1.4 copy-done.2
  67.2 2.3 copy_bitcast_fusion.1
  69.6 0.0 reduce-scatter.9.cloned.1.call-start
  69.6 25.8 %reduce-scatter.7.cloned.1.call-done = f32[128,512]{1,0:T(8,128)} async-done(((f32[512,512]{1,0:T(8,128)}), f32[128,512]{1,0:T(8,128)}) %reduce-scatter.7.cloned.1.call-update) | async-done | bytes 262160 | tf_op jit(solution)/shard_map/reduce_scatter | solution.py:170
  95.4 1.0 convert_element_type.49
  96.4 8.1 %convolution_bitcast_fusion.1 = f32[8192,512]{0,1:T(8,128)} fusion(bf16[128,512]{1,0:T(8,128)(2,1)S(1)} %convert_element_type.49, bf16[128,8192]{1,0:T(8,128)(2,1)S(1)} %copy-done), kind=kOutput, calls=%fused_computation.58 | convolution fusion | flops 1073741824 | bytes 19005440 | tf_op jit(solution)/shard_map/dot_general | solution.py:194
  104.6 0.0 reduce-scatter.5.cloned.1.call-start
  104.6 1.1 copy-done.8
  105.8 1.3 copy.35
  107.1 0.3 reduce-scatter.11.cloned.1.call-start
  107.4 122.3 %reduce-scatter.9.cloned.1.call-done = f32[2048,512]{0,1:T(8,128)} async-done(((f32[8192,512]{0,1:T(8,128)}), f32[2048,512]{0,1:T(8,128)}) %reduce-scatter.9.cloned.1.call-update) | async-done | bytes 4194320 | tf_op jit(solution)/shard_map/reduce_scatter | solution.py:193
  229.7 0.1 copy.34
  229.8 3.0 fusion.47
  232.8 2.7 subtract_convert_fusion
  235.5 0.6 pad_maximum_fusion.1
  236.1 1.4 copy.58
  237.5 19.5 %reduce-scatter.5.cloned.1.call-done = f32[128,512]{0,1:T(8,128)} async-done(((f32[512,512]{0,1:T(8,128)}), f32[128,512]{0,1:T(8,128)}) %reduce-scatter.5.cloned.1.call-update) | async-done | bytes 262160 | tf_op jit(solution)/shard_map/reduce_scatter | solution.py:164
  257.0 1.0 subtract_convert_fusion.2
  258.1 0.8 copy.45
  258.8 90.6 %reduce-scatter.11.cloned.1.call-done = f32[2048,64]{0,1:T(8,128)} async-done(((f32[2048,512]{0,1:T(8,128)}), f32[2048,64]{0,1:T(8,128)}) %reduce-scatter.11.cloned.1.call-update) | async-done | bytes 524304 | tf_op jit(solution)/shard_map/reduce_scatter | solution.py:201
  (54 shorter events, 0.3 us)
Async XLA Ops:
  7.2 89.2 %copy-start = (bf16[128,8192]{1,0:T(8,128)(2,1)S(1)}, bf16[128,8192]{1,0:T(8,128)(2,1)}, u32[]{:S(2)}) copy-start(bf16[128,8192]{1,0:T(8,128)(2,1)} %param.17) | copy-start | bytes 6291460
  7.2 88.3 %reduce-scatter.7.cloned.1.call-start = ((), (), s32[]{:S(2)}) async-start(), calls=%async_computation.5 | async-start | bytes 1310720 | tf_op jit(solution)/shard_map/reduce_scatter | solution.py:170
  17.9 2.3 copy-start.16
  18.0 22.9 %copy-start.13 = (f32[128,64]{1,0:T(8,128)}, f32[128,64]{1,0:T(8,128)S(1)}, u32[]{:S(2)}) copy-start(f32[128,64]{1,0:T(8,128)S(1)} %copy.20) | copy-start | bytes 98308
  46.5 1.8 copy-start.3
  46.5 1.8 copy-start.11
  55.4 3.4 copy-start.4
  55.4 3.4 copy-start.9
  58.8 1.3 copy-start.12
  60.2 1.3 copy-start.10
  60.2 1.6 copy-start.6
  61.8 1.6 copy-start.1
  61.8 1.7 copy-start.5
  63.5 2.4 copy-start.7
  65.9 1.4 copy-start.2
  69.6 160.1 %reduce-scatter.9.cloned.1.call-start = ((), (), s32[]{:S(2)}) async-start(), calls=%async_computation.6 | async-start | bytes 20971520 | tf_op jit(solution)/shard_map/reduce_scatter | solution.py:193
  96.4 8.1 %copy-start.15 = (bf16[128,512]{1,0:T(8,128)(2,1)}, bf16[128,512]{1,0:T(8,128)(2,1)S(1)}, u32[]{:S(2)}) copy-start(bf16[128,512]{1,0:T(8,128)(2,1)S(1)} %convert_element_type.49) | copy-start | bytes 393220
  104.5 1.2 copy-start.8
  104.6 125.1 %copy-start.18 = (f32[128,64]{0,1:T(8,128)S(1)}, f32[128,64]{0,1:T(8,128)}, u32[]{:S(2)}) copy-start(f32[128,64]{0,1:T(8,128)} %get-tuple-element.322) | copy-start | bytes 98308
  104.6 152.4 %reduce-scatter.5.cloned.1.call-start = ((), (), s32[]{:S(2)}) async-start(), calls=%async_computation.4 | async-start | bytes 1310720 | tf_op jit(solution)/shard_map/reduce_scatter | solution.py:164
  107.1 242.3 %reduce-scatter.11.cloned.1.call-start = ((), (), s32[]{:S(2)}) async-start(), calls=%async_computation.7 | async-start | bytes 4718592 | tf_op jit(solution)/shard_map/reduce_scatter | solution.py:201
  229.8 3.0 copy-start.14
  235.5 21.5 %copy-start.17 = (f32[128,64]{0,1:T(8,128)S(1)}, f32[128,64]{0,1:T(8,128)}, u32[]{:S(2)}) copy-start(f32[128,64]{0,1:T(8,128)} %copy-done.16) | copy-start | bytes 98308
Sparse Core Ops, SparseCore 0:
  69.7 25.6 reduce-scatter.6
  104.7 124.9 reduce-scatter.8
  232.2 24.7 reduce-scatter.4
  261.1 88.2 reduce-scatter.10
where the time goes:
time: 357 us; the launch traced here: 356 us
  waiting for transfers between devices  258 us (72%)
  local copies, waits for them, and re-layouts  26.1 us (7%)
  matrix products  22.7 us (6%)
  blocking collectives  20.3 us (6%)
  between operations  14.8 us (4%)
  other arithmetic  13.3 us (4%)
    reduce_scatter x1, waiting for transfers between devices, per_device(): lax.psum_scatter(lax.dot_general(inputs, value_grad, (((0,), (0,)), ((),...  122 us
    reduce_scatter x1, waiting for transfers between devices, per_device(): lax.psum_scatter(weight_part, 'dp', scatter_dimension=1, tiled=True)  90.6 us
    reduce_scatter x1, waiting for transfers between devices, per_device(): lax.psum_scatter(value_accumulator.reshape(retained_slots, KEY_HEADS * HE...  25.8 us
    reduce_scatter x1, waiting for transfers between devices, per_device(): lax.psum_scatter(key_accumulator.reshape(retained_slots, KEY_HEADS * HEAD...  19.5 us
    unnamed x26, local copies, waits for them, and re-layouts  10.9 us
    dot_general x1, matrix products, per_device(): lax.dot_general(inputs, value_grad, (((0,), (0,)), ((), ())), preferred_e...  8.12 us
    all_gather x1, blocking collectives, per_device(): lax.all_gather(value_head_inputs, 'ctx', axis=0, tiled=True)  7.29 us
  transfers between devices with their start and end apart: 4, of which 4 were waited for; matrix products, arithmetic and copies ran while one was open for 3% of the time, Pallas kernels for 0%

commit v1 on v0

--- a/solution.py
+++ b/solution.py
@@ -58,9 +58,37 @@
         1.0,
     ).astype(jnp.bfloat16)
     key_rotated = key_rotated.reshape(row_number_total, KEY_HEADS * HEAD_DIM)
+
+    def stacks_all_serve(field, axis_k):
+        answer, val2, x_new = (lax.axis_size("ctx"), lax.axis_index("ctx"), field.shape[axis_k])
+        entries = []
+        for kk, it in enumerate(field.shape):
+            entries.append(it * answer if kk == axis_k else it)
+        piece_now = lax.dynamic_update_slice_in_dim(
+            jnp.zeros(entries, field.dtype), field, val2 * x_new, axis=axis_k
+        )
+        work_now = block_now = field
+        for pp in range(1, answer // 2 + 1):
+            rows = []
+            for kk in range(answer):
+                rows.append((kk, (kk + 1) % answer))
+            work_now = lax.ppermute(work_now, axis_name="ctx", perm=rows)
+            piece_now = lax.dynamic_update_slice_in_dim(
+                piece_now, work_now, (val2 - pp) % answer * x_new, axis=axis_k
+            )
+            if 2 * pp < answer:
+                blocks_here = []
+                for kk in range(answer):
+                    blocks_here.append((kk, (kk - 1) % answer))
+                block_now = lax.ppermute(block_now, axis_name="ctx", perm=blocks_here)
+                piece_now = lax.dynamic_update_slice_in_dim(
+                    piece_now, block_now, (val2 + pp) % answer * x_new, axis=axis_k
+                )
+        return piece_now
+
     key_row_block, value_row_block, all_counts = (
         lax.all_gather(key_rotated, "ctx", axis=0, tiled=True),
-        lax.all_gather(value_head_inputs, "ctx", axis=0, tiled=True),
+        stacks_all_serve(value_head_inputs, 0),
         lax.all_gather(counts, "ctx", axis=0, tiled=True),
     )
     gathered_keys = key_row_block.reshape(retained_slots, KEY_HEADS, HEAD_DIM)

time: 357 us -> 364 us (1.020)
  local copies, waits for them, and re-layouts: 26.1 us -> 34.7 us
  blocking collectives: 20.3 us -> 12.8 us
    all_gather x1 -> x0, blocking collectives: 7.29 us -> none  [per_device(): lax.all_gather(value_head_inputs, 'ctx', axis=0, tiled=True)]
    unnamed x26 -> x28, local copies, waits for them, and re-layouts: 10.9 us -> 14.1 us
  transfers between devices with their start and end apart: 4 -> 7, of which waited for: 4 -> 5; matrix products, arithmetic and copies ran while one was open for 3% -> 9% of each run, Pallas kernels for 0% -> 0%
where the time goes in v1:
time: 364 us
  waiting for transfers between devices  261 us (72%)
  local copies, waits for them, and re-layouts  34.7 us (10%)
  matrix products  22.7 us (6%)
  other arithmetic  14.8 us (4%)
  between operations  14.7 us (4%)
  blocking collectives  12.8 us (4%)
    reduce_scatter x1, waiting for transfers between devices, per_device(): lax.psum_scatter(lax.dot_general(inputs, value_grad, (((0,), (0,)), ((),...  122 us
    reduce_scatter x1, waiting for transfers between devices, per_device(): lax.psum_scatter(weight_part, 'dp', scatter_dimension=1, tiled=True)  90.6 us
    reduce_scatter x1, waiting for transfers between devices, per_device(): lax.psum_scatter(value_accumulator.reshape(retained_slots, KEY_HEADS * HE...  25.5 us
    reduce_scatter x1, waiting for transfers between devices, per_device(): lax.psum_scatter(key_accumulator.reshape(retained_slots, KEY_HEADS * HEAD...  19.5 us
    unnamed x28, local copies, waits for them, and re-layouts  14.1 us
    all_gather x1, blocking collectives, per_device(): lax.all_gather(key_rotated, 'ctx', axis=0, tiled=True)  8.12 us
    dot_general x1, matrix products, per_device(): lax.dot_general(inputs, value_grad, (((0,), (0,)), ((), ())), preferred_e...  8.1 us
  transfers between devices with their start and end apart: 7, of which 5 were waited for; matrix products, arithmetic and copies ran while one was open for 9% of the time, Pallas kernels for 0%

profile of v1, /device:TPU:0, one launch (start us, length us, event | category | flops | bytes accessed | tf_op | source)
XLA Modules:
  0.0 363.7 jit_solution(12168322071289810417)
XLA Ops:
  7.2 1.2 copy.24
  8.4 2.5 collective-permute-start.1
  10.9 0.7 convert_element_type.43
  11.5 0.8 broadcast_multiply_fusion
  12.3 0.1 copy.20
  12.5 0.1 copy.21
  12.5 1.0 copy.48
  13.6 8.1 %all_gather.7 = bf16[512,512]{0,1:T(8,128)(2,1)} all-gather(bf16[128,512]{0,1:T(8,128)(2,1)S(1)} %bitcast.174), channel_id=1, replica_groups=mesh['dp'=8,'ctx'=4] {'ctx'}, dimensions={0}, use_global_device_ids=true | all-gather | bytes 655360 | tf_op jit(solution)/shard_map/all_gather | solution.py:90
  21.7 1.4 convert_bitcast_fusion
  23.2 0.4 copy.52
  23.6 0.8 subtract_convert_fusion.1
  24.4 1.4 copy.22
  25.8 1.4 copy.23
  27.2 2.1 pad_maximum_fusion
  29.3 0.9 broadcast_in_dim.72
  30.1 0.7 constant_dynamic-update-slice_fusion.3
  31.5 0.6 dynamic-slice
  32.1 0.8 dynamic-update-slice
  32.8 4.6 %all-reduce = s32[4]{0:T(128)S(1)} all-reduce(s32[4]{0:T(128)S(1)} %dynamic-update-slice), channel_id=1, replica_groups=mesh['dp'=8,'ctx'=4] {'ctx'}, use_global_device_ids=true, to_apply=%add | all-reduce | flops 4 | bytes 32
  37.5 2.0 copy.31
  39.5 2.3 copy.27
  41.8 2.3 copy.30
  44.1 0.7 constant_dynamic-update-slice_fusion.2
  44.8 0.7 constant_dynamic-update-slice_fusion.1
  45.4 3.0 collective-permute-done.2
  48.5 0.7 constant_dynamic-update-slice_fusion
  49.1 2.0 copy.29
  51.2 7.6 %while.30 = (s32[]{:T(128)}, f32[4,8,128]{2,1,0:T(8,128)S(1)}, f32[4,8,128]{2,1,0:T(8,128)S(1)}, f32[4,8,128]{2,1,0:T(8,128)S(1)}, s32[]{:T(128)}, /*index=5*/bf...) while((s32[]{:T(128)}, f32[4,8,128]{2,1,0:T(8,128)S(1)}, ...), condition=%wide.region_4.5_spmd.clone, body=%wide.region_0.4_spmd.clone.sunk | while | flops 1099120896 | bytes 35166692 | solution.py:145
  51.3 0.6 iota_compare_fusion.5
  52.0 0.2 compare_and_fusion.4
  52.2 2.3 fusion.85
  54.5 1.8 fusion.87
  56.3 2.4 fusion.86
  58.8 1.0 broadcast_in_dim.69.clone
  59.9 1.0 broadcast_in_dim.69
  60.9 1.6 broadcast_in_dim.68
  62.5 12.7 %while.31 = (s32[]{:T(128)}, f32[128,4,8,128]{3,0,2,1:T(8,128)}, f32[512,4,128]{2,0,1:T(8,128)}, f32[512,4,128]{2,0,1:T(8,128)}, s32[]{:T(128)}, /*index=5*/bf16...) while((s32[]{:T(128)}, f32[128,4,8,128]{3,0,2,1:T(8,128)}, ...), condition=%wide.region_6.7_spmd.clone, body=%wide.region_5.6_spmd.clone.sunk | while | flops 2704478464 | bytes 94034632 | solution.py:183
  62.6 0.6 iota_compare_fusion.6
  63.2 0.2 compare_and_fusion.5
  63.5 3.4 fusion.99
  66.9 1.3 fusion.102
  68.2 1.3 fusion.100
  69.5 0.3 copy-done.6
  69.8 1.5 fusion.101
  71.3 0.1 copy-done.1
  71.5 2.4 bitcast_add_fusion.2
  73.9 1.3 copy-done.2
  75.2 2.4 copy_bitcast_fusion.1
  77.7 25.5 %reduce-scatter.7.cloned.1.call-done = f32[128,512]{1,0:T(8,128)} async-done(((f32[512,512]{1,0:T(8,128)}), f32[128,512]{1,0:T(8,128)}) %reduce-scatter.7.cloned.1.call-update) | async-done | bytes 262160 | tf_op jit(solution)/shard_map/reduce_scatter | solution.py:198
  103.1 1.0 convert_element_type.49
  104.1 8.1 %convolution_bitcast_fusion.1 = f32[8192,512]{0,1:T(8,128)} fusion(bf16[128,512]{1,0:T(8,128)(2,1)S(1)} %convert_element_type.49, bf16[128,8192]{1,0:T(8,128)(2,1)S(1)} %copy-done), kind=kOutput, calls=%fused_computation.58 | convolution fusion | flops 1073741824 | bytes 19005440 | tf_op jit(solution)/shard_map/dot_general | solution.py:222
  112.3 1.1 copy-done.8
  113.5 1.3 copy.37
  114.8 0.3 reduce-scatter.11.cloned.1.call-start
  115.1 122.3 %reduce-scatter.9.cloned.1.call-done = f32[2048,512]{0,1:T(8,128)} async-done(((f32[8192,512]{0,1:T(8,128)}), f32[2048,512]{0,1:T(8,128)}) %reduce-scatter.9.cloned.1.call-update) | async-done | bytes 4194320 | tf_op jit(solution)/shard_map/reduce_scatter | solution.py:221
  237.4 0.1 copy.36
  237.5 3.0 fusion.47
  240.5 2.7 subtract_convert_fusion
  243.2 0.6 pad_maximum_fusion.1
  243.8 1.4 copy.60
  245.2 19.5 %reduce-scatter.5.cloned.1.call-done = f32[128,512]{0,1:T(8,128)} async-done(((f32[512,512]{0,1:T(8,128)}), f32[128,512]{0,1:T(8,128)}) %reduce-scatter.5.cloned.1.call-update) | async-done | bytes 262160 | tf_op jit(solution)/shard_map/reduce_scatter | solution.py:192
  264.7 1.0 subtract_convert_fusion.2
  265.7 0.8 copy.47
  266.5 90.6 %reduce-scatter.11.cloned.1.call-done = f32[2048,64]{0,1:T(8,128)} async-done(((f32[2048,512]{0,1:T(8,128)}), f32[2048,64]{0,1:T(8,128)}) %reduce-scatter.11.cloned.1.call-update) | async-done | bytes 524304 | tf_op jit(solution)/shard_map/reduce_scatter | solution.py:229
  (66 shorter events, 0.7 us)
Async XLA Ops:
  7.2 97.0 %copy-start = (bf16[128,8192]{1,0:T(8,128)(2,1)S(1)}, bf16[128,8192]{1,0:T(8,128)(2,1)}, u32[]{:S(2)}) copy-start(bf16[128,8192]{1,0:T(8,128)(2,1)} %param.17) | copy-start | bytes 6291460
  7.2 96.0 %reduce-scatter.7.cloned.1.call-start = ((), (), s32[]{:S(2)}) async-start(), calls=%async_computation.5 | async-start | bytes 1310720 | tf_op jit(solution)/shard_map/reduce_scatter | solution.py:198
  8.4 36.4 %collective-permute-start.1 = (bf16[128,512]{0,1:T(8,128)(2,1)S(1)}, bf16[128,512]{0,1:T(8,128)(2,1)S(1)}, u32[]{:S(2)}, u32[]{:S(2)}) collective-permute-start(bf16[128,512]{0,1:T(8,128)(2,1)S(1)} %copy.24), channel_id=1, source_target_pairs={{0,3},{1,0},{2,1},{3,2},{4,7},{5,4},{6,5},{7,6},{8,11},{9,8},{10,9... | collective-permute-start | bytes 393224 | tf_op jit(solution)/shard_map/ppermute | solution.py:83
  10.8 33.2 %collective-permute-start = (bf16[128,512]{0,1:T(8,128)(2,1)S(1)}, bf16[128,512]{0,1:T(8,128)(2,1)S(1)}, u32[]{:S(2)}, u32[]{:S(2)}) collective-permute-start(bf16[128,512]{0,1:T(8,128)(2,1)S(1)} %copy.24), channel_id=1, source_target_pairs={{0,1},{1,2},{2,3},{3,0},{4,5},{5,6},{6,7},{7,4},{8,9},{9,10},{10,1... | collective-permute-start | bytes 393224 | tf_op jit(solution)/shard_map/ppermute | solution.py:75
  12.3 11.2 %copy-start.16 = (f32[128,64]{0,1:T(8,128)}, f32[128,64]{0,1:T(8,128)S(1)}, u32[]{:S(2)}) copy-start(f32[128,64]{0,1:T(8,128)S(1)} %get-tuple-element.324) | copy-start | bytes 98308
  12.4 11.1 %copy-start.13 = (f32[128,64]{1,0:T(8,128)}, f32[128,64]{1,0:T(8,128)S(1)}, u32[]{:S(2)}) copy-start(f32[128,64]{1,0:T(8,128)S(1)} %copy.20) | copy-start | bytes 98308
  24.4 7.1 %copy-start.19 = (u32[32]{0:T(128)S(1)}, u32[32]{0:T(128)}, u32[]{:S(2)}) copy-start(u32[32]{0:T(128)} %constant.103) | copy-start | bytes 388
  44.1 4.4 %collective-permute-start.2 = (bf16[128,512]{0,1:T(8,128)(2,1)S(1)}, bf16[128,512]{0,1:T(8,128)(2,1)S(1)}, u32[]{:S(2)}, u32[]{:S(2)}) collective-permute-start(bf16[128,512]{0,1:T(8,128)(2,1)S(1)} %collective-permute-done), channel_id=1, source_target_pairs={{0,1},{1,2},{2,3},{3,0},{4,5},{5,6},{6,7},{7,4},{8,9},{9,10},{10,1... | collective-permute-start | bytes 393224 | tf_op jit(solution)/shard_map/ppermute | solution.py:75
  54.5 1.8 copy-start.3
  54.5 1.8 copy-start.11
  63.4 3.4 copy-start.4
  63.5 3.4 copy-start.9
  66.8 1.3 copy-start.12
  68.2 1.3 copy-start.10
  68.2 1.6 copy-start.6
  69.8 1.6 copy-start.1
  69.8 1.7 copy-start.5
  71.5 2.4 copy-start.7
  73.9 1.3 copy-start.2
  77.6 159.7 %reduce-scatter.9.cloned.1.call-start = ((), (), s32[]{:S(2)}) async-start(), calls=%async_computation.6 | async-start | bytes 20971520 | tf_op jit(solution)/shard_map/reduce_scatter | solution.py:221
  104.1 8.1 %copy-start.15 = (bf16[128,512]{1,0:T(8,128)(2,1)}, bf16[128,512]{1,0:T(8,128)(2,1)S(1)}, u32[]{:S(2)}) copy-start(bf16[128,512]{1,0:T(8,128)(2,1)S(1)} %convert_element_type.49) | copy-start | bytes 393220
  112.2 1.2 copy-start.8
  112.3 125.1 %copy-start.18 = (f32[128,64]{0,1:T(8,128)S(1)}, f32[128,64]{0,1:T(8,128)}, u32[]{:S(2)}) copy-start(f32[128,64]{0,1:T(8,128)} %get-tuple-element.322) | copy-start | bytes 98308
  112.3 152.4 %reduce-scatter.5.cloned.1.call-start = ((), (), s32[]{:S(2)}) async-start(), calls=%async_computation.4 | async-start | bytes 1310720 | tf_op jit(solution)/shard_map/reduce_scatter | solution.py:192
  114.8 242.4 %reduce-scatter.11.cloned.1.call-start = ((), (), s32[]{:S(2)}) async-start(), calls=%async_computation.7 | async-start | bytes 4718592 | tf_op jit(solution)/shard_map/reduce_scatter | solution.py:229
  237.5 3.0 copy-start.14
  243.2 21.5 %copy-start.17 = (f32[128,64]{0,1:T(8,128)S(1)}, f32[128,64]{0,1:T(8,128)}, u32[]{:S(2)}) copy-start(f32[128,64]{0,1:T(8,128)} %copy-done.16) | copy-start | bytes 98308
Sparse Core Ops, SparseCore 0:
  77.7 25.3 reduce-scatter.6
  112.4 124.9 reduce-scatter.8
  239.9 24.7 reduce-scatter.4
  268.8 88.3 reduce-scatter.10
